TPU v7x, 32 devices: a whole 2x2x4 slice. The times are simulated.
32 devices in a mesh: pole: 2 (over x), row: 8 (over z, y), col: 2 (over core).
Axes of the slice: x: 2, y: 2, z: 4, core: 2. Of those that a mesh axis runs over, the one named last changes fastest.
Arguments:
- anc_inverse: bfloat16 [2048, 1024], P(('pole', 'row')), parts along dimension 0, as said below
- parent_pivinv: float32 [2048, 1024], P(('pole', 'row')), parts along dimension 0, as said below
- parent_lower: bfloat16 [2048, 1024], P(('pole', 'row')), parts along dimension 0, may hold values from -0.1875 to 0.1875
- parent_mask: int32 [4], replicated, may hold values 0 or 1
- leaf_lower_par: bfloat16 [2048, 1024], P(('pole', 'row')), parts along dimension 0, may hold values from -0.125 to 0.125
- leaf_lower_anc: bfloat16 [2048, 1024], P(('pole', 'row')), parts along dimension 0, may hold values from -0.125 to 0.125
- leaf_mask: int32 [8], replicated, may hold values 0 or 1
- leaf_pivots: float32 [2048], P(('pole', 'col')), parts along dimension 0, may hold values from 0.5 to 2
Outputs:
- parent_block: float32 [2048, 1024], P(('pole', 'row')), parts along dimension 0
- parent_offdiag: bfloat16 [2048, 1024], P(('pole', 'row'), 'col'), parts along dimension 0
- leaf_par_block: bfloat16 [2048, 1024], P(('pole', 'row'), 'col'), parts along dimension 0
- leaf_anc_block: bfloat16 [2048, 1024], P(('pole', 'row'), 'col'), parts along dimension 0
- density: float32 [2048], P(('pole', 'col')), parts along dimension 0
There are 2 independent parts, one for each index of `pole`. A program takes and returns all parts, laid end to end along the dimension named above; an argument that names none is the same for every part. Nothing has to cross between parts.
Inputs may be any that keep to these rules, and one draw needn't show every extreme that they name: `anc_inverse`: symmetric. `parent_pivinv`: symmetric. `parent_mask`: 1 marks a structurally nonzero block of 256 rows. `leaf_mask`: 1 marks a structurally nonzero block of 256 rows.
All inputs are finite; a program needn't handle non-finite values.
Results may differ from a plain program's by a relative error of at most 0.0095.
Values may be sent and summed in bfloat16 or wider, within the bound.
No kernel may reach another device: no remote copies, remote signals or barrier semaphores. Data moves between devices by JAX's collectives and lax.ppermute only.
A program may use at most 64 MiB of HBM per device.

v0:
```python
import jax
import jax.numpy as jnp
from jax import lax
from jax.sharding import PartitionSpec as P

BLOCK = 256
ORDER = 1024


def local(
    anc_inverse,
    parent_pivinv,
    parent_lower,
    parent_mask,
    leaf_lower_par,
    leaf_lower_anc,
    leaf_mask,
    leaf_pivots,
):
    row_index = lax.axis_index("row")
    row_devices = lax.axis_size("row")
    col_index = lax.axis_index("col")
    anc_rows = anc_inverse.shape[0]
    order_rows = parent_pivinv.shape[0]
    col_width = leaf_pivots.shape[0]
    parent_gate = lax.dynamic_slice_in_dim(
        jnp.repeat(parent_mask, BLOCK), row_index * anc_rows, anc_rows
    )
    lower_one = parent_lower * parent_gate[:, None].astype(jnp.bfloat16)
    lower_half = lax.dynamic_slice_in_dim(lower_one, col_index * col_width, col_width, 1)
    leaf_gate = jnp.repeat(leaf_mask, BLOCK)
    gate_par = lax.dynamic_slice_in_dim(leaf_gate[:ORDER], row_index * order_rows, order_rows)
    gate_anc = lax.dynamic_slice_in_dim(leaf_gate[ORDER:], row_index * anc_rows, anc_rows)
    leaf_local = jnp.concatenate(
        [
            leaf_lower_par * gate_par[:, None].astype(jnp.bfloat16),
            leaf_lower_anc * gate_anc[:, None].astype(jnp.bfloat16),
        ],
        axis=0,
    )
    leaf_half = lax.dynamic_slice_in_dim(leaf_local, col_index * col_width, col_width, 1)
    columns = anc_inverse
    product = jnp.dot(
        columns,
        lax.all_gather(lower_half, "row", axis=0, tiled=True),
        preferred_element_type=jnp.float32,
    )
    parent_offdiag = (-product).astype(jnp.bfloat16)
    offdiag_rows = lax.all_gather(parent_offdiag, "col", axis=1, tiled=True)
    columns = lower_one
    diag_sums = lax.psum_scatter(
        lax.dot_general(
            columns, offdiag_rows, (((0,), (0,)), ((), ())), preferred_element_type=jnp.float32
        ),
        "row",
        scatter_dimension=0,
        tiled=True,
    )
    parent_block = parent_pivinv - diag_sums
    parent_round = parent_block.astype(jnp.bfloat16)
    mirrored = lax.all_to_all(offdiag_rows, "row", split_axis=1, concat_axis=0, tiled=True).T
    upper_rows = jnp.concatenate(
        [
            parent_round.reshape(order_rows, row_devices, order_rows),
            mirrored.reshape(order_rows, row_devices, anc_rows),
        ],
        axis=2,
    )
    lower_rows = jnp.concatenate(
        [
            offdiag_rows.reshape(anc_rows, row_devices, order_rows),
            anc_inverse.reshape(anc_rows, row_devices, anc_rows),
        ],
        axis=2,
    )
    inverse_rows = jnp.concatenate(
        [upper_rows.reshape(order_rows, -1), lower_rows.reshape(anc_rows, -1)], axis=0
    )
    columns = inverse_rows
    leaf_product = jnp.dot(
        columns,
        lax.all_gather(leaf_half, "row", axis=0, tiled=True),
        preferred_element_type=jnp.float32,
    )
    leaf_result = (-leaf_product).astype(jnp.bfloat16)
    partial_sums = jnp.sum(leaf_half.astype(jnp.float32) * leaf_result.astype(jnp.float32), axis=0)
    density = leaf_pivots - lax.psum(partial_sums, "row")
    return (
        parent_block,
        parent_offdiag,
        leaf_result[:order_rows],
        leaf_result[order_rows:],
        density,
    )


def local_whole(
    anc_inverse,
    parent_pivinv,
    parent_lower,
    parent_mask,
    leaf_lower_par,
    leaf_lower_anc,
    leaf_mask,
    leaf_pivots,
):
    row_index = lax.axis_index("row")
    row_devices = lax.axis_size("row")
    col_index = lax.axis_index("col")
    anc_rows = anc_inverse.shape[0]
    order_rows = parent_pivinv.shape[0]
    col_width = leaf_pivots.shape[0]
    off_width = parent_lower.shape[1] // 2
    half = anc_rows // 2

    def mine(x):
        return lax.dynamic_slice_in_dim(x, col_index * half, half, 0)

    order_all = order_rows * row_devices
    parent_gate = jnp.repeat(parent_mask, BLOCK).astype(jnp.bfloat16)
    leaf_gate = jnp.repeat(leaf_mask, BLOCK).astype(jnp.bfloat16)
    anc_start = row_index * anc_rows + col_index * half
    order_start = row_index * order_rows + col_index * half
    lower_gate = lax.dynamic_slice_in_dim(parent_gate, anc_start, half)
    par_gate = lax.dynamic_slice_in_dim(leaf_gate[:order_all], order_start, half)
    anc_gate = lax.dynamic_slice_in_dim(leaf_gate[order_all:], anc_start, half)
    stacked = jnp.stack(
        [
            mine(anc_inverse),
            mine(parent_lower) * lower_gate[:, None],
            mine(leaf_lower_par) * par_gate[:, None],
            mine(leaf_lower_anc) * anc_gate[:, None],
        ]
    )
    full = lax.all_gather(stacked, ("row", "col"), axis=1, tiled=True)
    anc_full, lower_m, par_m, anc_m = (full[0], full[1], full[2], full[3])
    offdiag_all = (-jnp.dot(anc_full, lower_m, preferred_element_type=jnp.float32)).astype(
        jnp.bfloat16
    )
    lower_cols = lax.dynamic_slice_in_dim(lower_m, row_index * order_rows, order_rows, 1)
    parent_block = parent_pivinv - lax.dot_general(
        lower_cols, offdiag_all, (((0,), (0,)), ((), ())), preferred_element_type=jnp.float32
    )
    parent_round = parent_block.astype(jnp.bfloat16)
    par_half = lax.dynamic_slice_in_dim(par_m, col_index * col_width, col_width, 1)
    anc_half = lax.dynamic_slice_in_dim(anc_m, col_index * col_width, col_width, 1)
    offdiag_cols = lax.dynamic_slice_in_dim(offdiag_all, row_index * order_rows, order_rows, 1)
    offdiag_rows = lax.dynamic_slice_in_dim(offdiag_all, row_index * anc_rows, anc_rows, 0)
    upper_sum = jnp.dot(
        parent_round, par_half, preferred_element_type=jnp.float32
    ) + lax.dot_general(
        offdiag_cols, anc_half, (((0,), (0,)), ((), ())), preferred_element_type=jnp.float32
    )
    lower_sum = jnp.dot(offdiag_rows, par_half, preferred_element_type=jnp.float32) + jnp.dot(
        anc_inverse, anc_half, preferred_element_type=jnp.float32
    )
    leaf_par_block = (-upper_sum).astype(jnp.bfloat16)
    leaf_anc_block = (-lower_sum).astype(jnp.bfloat16)
    par_own = lax.dynamic_slice_in_dim(par_half, row_index * order_rows, order_rows, 0)
    anc_own = lax.dynamic_slice_in_dim(anc_half, row_index * anc_rows, anc_rows, 0)
    partial_sums = jnp.sum(
        par_own.astype(jnp.float32) * leaf_par_block.astype(jnp.float32), axis=0
    ) + jnp.sum(anc_own.astype(jnp.float32) * leaf_anc_block.astype(jnp.float32), axis=0)
    spread = jnp.broadcast_to(partial_sums[None], (row_devices, col_width))
    column_sums = jnp.sum(lax.all_to_all(spread, "row", 0, 0, tiled=True), axis=0)
    density = leaf_pivots - column_sums
    offdiag_own = lax.dynamic_slice_in_dim(offdiag_rows, col_index * off_width, off_width, 1)
    return (parent_block, offdiag_own, leaf_par_block, leaf_anc_block, density)


def fits_whole(mesh, anc_rows, order_rows, order_cols, leaf_cols):
    anc_all = anc_rows * mesh.shape["row"]
    return (
        anc_rows == order_rows
        and anc_rows % 2 == 0
        and (len({anc_all, order_cols, leaf_cols}) == 1)
        and (anc_all * anc_all * 2 <= 16 * 1024 * 1024)
    )


def solution(mesh):
    placed = (
        P(("pole", "row"), None),
        P(("pole", "row"), None),
        P(("pole", "row"), None),
        P(),
        P(("pole", "row"), None),
        P(("pole", "row"), None),
        P(),
        P(("pole", "col")),
    )
    placed_out = (
        P(("pole", "row"), None),
        P(("pole", "row"), "col"),
        P(("pole", "row"), "col"),
        P(("pole", "row"), "col"),
        P(("pole", "col")),
    )
    shards = mesh.shape["pole"] * mesh.shape["row"]

    def run(*args):
        anc_rows = args[0].shape[0] // shards
        order_rows = args[1].shape[0] // shards
        body = (
            local_whole
            if fits_whole(mesh, anc_rows, order_rows, args[2].shape[1], args[4].shape[1])
            else local
        )
        return jax.shard_map(
            body, mesh=mesh, in_specs=placed, out_specs=placed_out, check_vma=False
        )(*args)

    return run
```

profile of v0, /device:TPU:0, one launch (start us, length us, event | category | flops | bytes accessed | tf_op | source)
XLA Modules:
  0.0 118.8 jit_solution(13952267705256480365)
XLA Ops:
  7.2 0.0 all-gather.2.cloned.1.call-start
  7.2 0.7 convert_element_type.44
  7.9 0.1 fusion.30
  8.0 0.1 broadcast_bitcast_fusion.1
  8.0 0.1 broadcast_bitcast_fusion
  8.1 0.1 dynamic_slice.55
  8.2 0.1 dynamic_slice.57
  8.3 0.7 convert_element_type.42
  8.9 0.1 broadcast_bitcast_fusion.2
  9.0 0.1 dynamic_slice.53
  9.1 1.1 multiply_bitcast_fusion.2
  10.1 1.1 multiply_bitcast_fusion
  11.2 0.9 pad_maximum_fusion
  12.1 0.0 all-gather.2.cloned.1.call-update
  12.1 77.8 %all-gather.2.cloned.1.call-done = bf16[4,1024,1024]{2,1,0:T(8,128)(2,1)} async-done(((bf16[4,64,1024]{2,1,0:T(8,128)(2,1)}), bf16[4,1024,1024]{2,1,0:T(8,128)(2,1)}) %all-gather.2.cloned.1.call-update) | async-done | bytes 8388624 | tf_op jit(solution)/shard_map/all_gather | solution.py:135
  89.9 3.8 %fusion.29 = (bf16[1,1024,1024]{2,1,0:T(8,128)(2,1)S(1)}, bf16[1,1024,1024]{2,1,0:T(8,128)(2,1)S(1)}, bf16[1,1024,1024]{2,1,0:T(8,128)(2,1)S(1)}) fusion(bf16[4,1024,1024]{2,1,0:T(8,128)(2,1)} %all-gather.2.cloned.1.call-done), kind=kLoop, calls=%fused_computation.44 | loop fusion | bytes 12582912 | tf_op jit(solution)/shard_map/slice | solution.py:136
  93.7 1.5 %copy-done = bf16[4,1024,1024]{2,1,0:T(8,128)(2,1)S(1)} copy-done((bf16[4,1024,1024]{2,1,0:T(8,128)(2,1)S(1)}, bf16[4,1024,1024]{2,1,0:T(8,128)(2,1)}, u32[]{:S(2)}) %copy-start) | copy-done | bytes 8388632
  95.2 2.3 %negate_convert_fusion = bf16[1024,1024]{1,0:T(8,128)(2,1)S(1)} fusion(bf16[4,1024,1024]{2,1,0:T(8,128)(2,1)S(1)} %copy-done), kind=kOutput, calls=%fused_computation | convolution fusion | flops 2149580800 | bytes 6291456 | tf_op jit(solution)/shard_map/dot_general | solution.py:137
  97.5 0.3 fusion.8
  97.8 0.0 copy-start.2
  97.8 0.5 convolution_subtract_fusion
  98.3 0.0 copy-start.1
  98.3 0.3 fusion.10
  98.7 0.0 copy-start.4
  98.7 0.1 copy-done.2
  98.8 1.0 fusion.16
  99.8 1.1 fusion.17
  100.9 0.6 broadcast_in_dim.20
  101.5 3.3 %all-to-all-start = ((f32[8,1,512]{2,1,0:T(1,128)}), f32[8,1,512]{2,1,0:T(1,128)S(1)}, u32[]{:S(2)}, u32[]{:S(2)}) async-start(f32[8,1,512]{2,1,0:T(1,128)} %broadcast_in_dim.20), calls=%async_computation | async-start | bytes 32768 | tf_op jit(solution)/shard_map/all_to_all | solution.py:165
  104.8 0.8 dynamic_slice.60
  105.6 5.7 %all-to-all-done = f32[8,1,512]{2,1,0:T(1,128)S(1)} async-done(((f32[8,1,512]{2,1,0:T(1,128)}), f32[8,1,512]{2,1,0:T(1,128)S(1)}, u32[]{:S(2)}, u32[]{:S(2)}) %all-to-all-start) | async-done | bytes 16416 | tf_op jit(solution)/shard_map/all_to_all | solution.py:165
  111.3 0.6 sub.7
  (10 shorter events, 0.1 us)
Async XLA Ops:
  7.2 82.7 %all-gather.2.cloned.1.call-start = ((), (), s32[]{:S(2)}) async-start(), calls=%async_computation.1 | async-start | bytes 8912896 | tf_op jit(solution)/shard_map/all_gather | solution.py:135
  89.9 5.2 %copy-start = (bf16[4,1024,1024]{2,1,0:T(8,128)(2,1)S(1)}, bf16[4,1024,1024]{2,1,0:T(8,128)(2,1)}, u32[]{:S(2)}) copy-start(bf16[4,1024,1024]{2,1,0:T(8,128)(2,1)} %all-gather.2.cloned.1.call-done) | copy-start | bytes 25165828
  95.1 2.7 %copy-start.3 = (f32[128,1024]{1,0:T(8,128)S(1)}, f32[128,1024]{1,0:T(8,128)}, u32[]{:S(2)}) copy-start(f32[128,1024]{1,0:T(8,128)} %param.9) | copy-start | bytes 1572868
  97.8 1.0 copy-start.2
  98.3 2.5 %copy-start.1 = (f32[128,1024]{1,0:T(8,128)}, f32[128,1024]{1,0:T(8,128)S(1)}, u32[]{:S(2)}) copy-start(f32[128,1024]{1,0:T(8,128)S(1)} %convolution_subtract_fusion) | copy-start | bytes 1572868
  98.7 12.7 %copy-start.4 = (f32[512]{0:T(512)S(1)}, f32[512]{0:T(512)}, u32[]{:S(2)}) copy-start(f32[512]{0:T(512)} %param.15) | copy-start | bytes 6148
  101.5 9.8 %all-to-all-start = ((f32[8,1,512]{2,1,0:T(1,128)}), f32[8,1,512]{2,1,0:T(1,128)S(1)}, u32[]{:S(2)}, u32[]{:S(2)}) async-start(f32[8,1,512]{2,1,0:T(1,128)} %broadcast_in_dim.20), calls=%async_computation | async-start | bytes 32768 | tf_op jit(solution)/shard_map/all_to_all | solution.py:165
Sparse Core Ops, SparseCore 0:
  12.2 77.6 all-gather.1
where the time goes:
time: 119 us
  waiting for transfers between devices  83.5 us (70%)
  between operations  14.2 us (12%)
  local copies, waits for them, and re-layouts  7.3 us (6%)
  matrix products  5.52 us (5%)
  other arithmetic  4.94 us (4%)
  starting transfers between devices  3.36 us (3%)
    all_gather x1, waiting for transfers between devices, local_whole(): full = lax.all_gather(stacked, ('row', 'col'), axis=1, tiled=True)  77.8 us
    all_to_all x1, waiting for transfers between devices, local_whole(): lax.all_to_all(spread, 'row', 0, 0, tiled=True)  5.73 us
    slice x1, local copies, waits for them, and re-layouts, local_whole(): anc_full, lower_m, par_m, anc_m = (full[0], full[1], full[2], full[3])  3.75 us
    all_to_all x1, starting transfers between devices, local_whole(): lax.all_to_all(spread, 'row', 0, 0, tiled=True)  3.32 us
    another operation x3, other arithmetic, local_whole(): jnp.stack([mine(anc_inverse), mine(parent_lower) * lower_gate[:, None], m...  3 us
  transfers between devices with their start and end apart: 2, of which 2 were waited for; matrix products, arithmetic and copies ran while one was open for 1% of the time, Pallas kernels for 0%

commit v1 on v0

--- a/solution.py
+++ b/solution.py
@@ -132,7 +132,30 @@
             mine(leaf_lower_anc) * anc_gate[:, None],
         ]
     )
-    full = lax.all_gather(stacked, ("row", "col"), axis=1, tiled=True)
+    devices, here, extent = (
+        lax.axis_size(("row", "col")),
+        lax.axis_index(("row", "col")),
+        stacked.shape[1],
+    )
+    right = [(i, (i + 1) % devices) for i in range(devices)]
+    backward = [(i, (i - 1) % devices) for i in range(devices)]
+    result = jnp.zeros(
+        (*stacked.shape[:1], devices * extent, *stacked.shape[1 + 1 :]), stacked.dtype
+    )
+    result = lax.dynamic_update_slice_in_dim(result, stacked, here * extent, axis=1)
+    from_left = from_right = stacked
+    middle = devices // 2
+    for turn in range(1, middle + 1):
+        from_left = lax.ppermute(from_left, ("row", "col"), right)
+        result = lax.dynamic_update_slice_in_dim(
+            result, from_left, (here - turn) % devices * extent, axis=1
+        )
+        if turn < devices - middle:
+            from_right = lax.ppermute(from_right, ("row", "col"), backward)
+            result = lax.dynamic_update_slice_in_dim(
+                result, from_right, (here + turn) % devices * extent, axis=1
+            )
+    full = result
     anc_full, lower_m, par_m, anc_m = (full[0], full[1], full[2], full[3])
     offdiag_all = (-jnp.dot(anc_full, lower_m, preferred_element_type=jnp.float32)).astype(
         jnp.bfloat16

time: 119 us -> 143 us (1.20)
  starting transfers between devices: 3.36 us -> 68 us
  waiting for transfers between devices: 83.5 us -> 33.5 us
  local copies, waits for them, and re-layouts: 7.3 us -> 27.4 us
  between operations: 14.2 us -> 0.79 us
  matrix products: 5.52 us -> 7.82 us
    all_gather x1 -> x0, waiting for transfers between devices: 77.8 us -> none  [local_whole(): full = lax.all_gather(stacked, ('row', 'col'), axis=1, tiled=True)]
    ppermute x0 -> x15, starting transfers between devices: none -> 60.1 us  [the longest x8 52.9 us: local_whole(): from_left = lax.ppermute(from_left, ('row', 'col'), right)]
    ppermute x0 -> x15, waiting for transfers between devices: none -> 27.7 us  [the longest x8 27.7 us: local_whole(): from_left = lax.ppermute(from_left, ('row', 'col'), right)]
    dynamic_update_slice x0 -> x15, local copies, waits for them, and re-layouts: none -> 17.5 us  [the longest x8 10.8 us: local_whole(): lax.dynamic_update_slice_in_dim(result, from_left, (here - turn) % device...]
    all_to_all x1, starting transfers between devices: 3.32 us -> 7.98 us  [local_whole(): lax.all_to_all(spread, 'row', 0, 0, tiled=True)]
    broadcast_in_dim x0 -> x1, local copies, waits for them, and re-layouts: none -> 4.32 us  [local_whole(): jnp.zeros((*stacked.shape[:1], devices * extent, *stacked.shape[1 + 1:]),...]
    dot_general x1, matrix products: 2.33 us -> 4.62 us  [local_whole(): jnp.dot(anc_full, lower_m, preferred_element_type=jnp.float32)]
    unnamed x16 -> x18, local copies, waits for them, and re-layouts: 1.85 us -> 0.27 us
  transfers between devices with their start and end apart: 2 -> 16, of which waited for: 2 -> 6; matrix products, arithmetic and copies ran while one was open for 1% -> 12% of each run, Pallas kernels for 0% -> 0%
where the time goes in v1:
time: 143 us
  starting transfers between devices  68 us (48%)
  waiting for transfers between devices  33.5 us (23%)
  local copies, waits for them, and re-layouts  27.4 us (19%)
  matrix products  7.82 us (5%)
  other arithmetic  4.97 us (3%)
    ppermute x8, starting transfers between devices, local_whole(): from_left = lax.ppermute(from_left, ('row', 'col'), right)  52.9 us
    ppermute x8, waiting for transfers between devices, local_whole(): from_left = lax.ppermute(from_left, ('row', 'col'), right)  27.7 us
    dynamic_update_slice x8, local copies, waits for them, and re-layouts, local_whole(): lax.dynamic_update_slice_in_dim(result, from_left, (here - turn) % device...  10.8 us
    all_to_all x1, starting transfers between devices, local_whole(): lax.all_to_all(spread, 'row', 0, 0, tiled=True)  7.98 us
    ppermute x7, starting transfers between devices, local_whole(): from_right = lax.ppermute(from_right, ('row', 'col'), backward)  7.17 us
    dynamic_update_slice x7, local copies, waits for them, and re-layouts, local_whole(): lax.dynamic_update_slice_in_dim(result, from_right, (here + turn) % devic...  6.78 us
    all_to_all x1, waiting for transfers between devices, local_whole(): lax.all_to_all(spread, 'row', 0, 0, tiled=True)  5.8 us
    dot_general x1, matrix products, local_whole(): jnp.dot(anc_full, lower_m, preferred_element_type=jnp.float32)  4.62 us
  transfers between devices with their start and end apart: 16, of which 6 were waited for; matrix products, arithmetic and copies ran while one was open for 12% of the time, Pallas kernels for 0%

profile of v1, /device:TPU:0, one launch (start us, length us, event | category | flops | bytes accessed | tf_op | source)
XLA Modules:
  0.0 142.6 jit_solution(5554757479583187245)
XLA Ops:
  2.5 1.1 multiply_bitcast_fusion.2
  3.6 1.1 multiply_bitcast_fusion
  4.7 4.3 %broadcast_in_dim.20 = bf16[4,1024,1024]{2,1,0:T(8,128)(2,1)} broadcast(bf16[]{:T(256)} %constant.140.clone.1), dimensions={} | broadcast | bytes 8388610 | tf_op jit(solution)/shard_map/broadcast_in_dim | solution.py:142
  9.0 0.9 pad_maximum_fusion
  10.3 5.0 %collective-permute-start.1 = (bf16[4,64,1024]{2,1,0:T(8,128)(2,1)S(1)}, bf16[4,64,1024]{2,1,0:T(8,128)(2,1)S(1)}, u32[]{:S(2)}, u32[]{:S(2)}) collective-permute-start(bf16[4,64,1024]{2,1,0:T(8,128)(2,1)S(1)} %get-tuple-element.8), channel_id=1, source_target_pairs={{0,15},{1,0},{2,1},{3,2},{4,3},{5,4},{6,5},{7,6},{8,7},{9,8},{10,9... | collective-permute-start | bytes 1572872 | tf_op jit(solution)/shard_map/ppermute | solution.py:154
  15.4 7.0 %collective-permute-done = bf16[4,64,1024]{2,1,0:T(8,128)(2,1)S(1)} collective-permute-done((bf16[4,64,1024]{2,1,0:T(8,128)(2,1)S(1)}, bf16[4,64,1024]{2,1,0:T(8,128)(2,1)S(1)}, u32[]{:S(2)}, u32[]{:S(2)}) %collective-permute-start) | collective-permute-done | bytes 524320 | tf_op jit(solution)/shard_map/ppermute | solution.py:149
  22.3 2.4 %collective-permute-start.2 = (bf16[4,64,1024]{2,1,0:T(8,128)(2,1)S(1)}, bf16[4,64,1024]{2,1,0:T(8,128)(2,1)S(1)}, u32[]{:S(2)}, u32[]{:S(2)}) collective-permute-start(bf16[4,64,1024]{2,1,0:T(8,128)(2,1)S(1)} %collective-permute-done), channel_id=1, source_target_pairs={{0,1},{1,2},{2,3},{3,4},{4,5},{5,6},{6,7},{7,8},{8,9},{9,10},{10,1... | collective-permute-start | bytes 1572872 | tf_op jit(solution)/shard_map/ppermute | solution.py:149
  24.7 2.0 %collective-permute-start.3 = (bf16[4,64,1024]{2,1,0:T(8,128)(2,1)S(1)}, bf16[4,64,1024]{2,1,0:T(8,128)(2,1)S(1)}, u32[]{:S(2)}, u32[]{:S(2)}) collective-permute-start(bf16[4,64,1024]{2,1,0:T(8,128)(2,1)S(1)} %collective-permute-done.1), channel_id=1, source_target_pairs={{0,15},{1,0},{2,1},{3,2},{4,3},{5,4},{6,5},{7,6},{8,7},{9,8},{10,9... | collective-permute-start | bytes 1572872 | tf_op jit(solution)/shard_map/ppermute | solution.py:154
  26.8 7.0 %collective-permute-done.2 = bf16[4,64,1024]{2,1,0:T(8,128)(2,1)S(1)} collective-permute-done((bf16[4,64,1024]{2,1,0:T(8,128)(2,1)S(1)}, bf16[4,64,1024]{2,1,0:T(8,128)(2,1)S(1)}, u32[]{:S(2)}, u32[]{:S(2)}) %collective-permute-start.2) | collective-permute-done | bytes 524320 | tf_op jit(solution)/shard_map/ppermute | solution.py:149
  33.8 4.4 %collective-permute-start.4 = (bf16[4,64,1024]{2,1,0:T(8,128)(2,1)S(1)}, bf16[4,64,1024]{2,1,0:T(8,128)(2,1)S(1)}, u32[]{:S(2)}, u32[]{:S(2)}) collective-permute-start(bf16[4,64,1024]{2,1,0:T(8,128)(2,1)S(1)} %collective-permute-done.2), channel_id=1, source_target_pairs={{0,1},{1,2},{2,3},{3,4},{4,5},{5,6},{6,7},{7,8},{8,9},{9,10},{10,1... | collective-permute-start | bytes 1572872 | tf_op jit(solution)/shard_map/ppermute | solution.py:149
  38.2 7.0 %collective-permute-done.4 = bf16[4,64,1024]{2,1,0:T(8,128)(2,1)S(1)} collective-permute-done((bf16[4,64,1024]{2,1,0:T(8,128)(2,1)S(1)}, bf16[4,64,1024]{2,1,0:T(8,128)(2,1)S(1)}, u32[]{:S(2)}, u32[]{:S(2)}) %collective-permute-start.4) | collective-permute-done | bytes 524320 | tf_op jit(solution)/shard_map/ppermute | solution.py:149
  45.2 6.5 %collective-permute-start.6 = (bf16[4,64,1024]{2,1,0:T(8,128)(2,1)S(1)}, bf16[4,64,1024]{2,1,0:T(8,128)(2,1)S(1)}, u32[]{:S(2)}, u32[]{:S(2)}) collective-permute-start(bf16[4,64,1024]{2,1,0:T(8,128)(2,1)S(1)} %collective-permute-done.4), channel_id=1, source_target_pairs={{0,1},{1,2},{2,3},{3,4},{4,5},{5,6},{6,7},{7,8},{8,9},{9,10},{10,1... | collective-permute-start | bytes 1572872 | tf_op jit(solution)/shard_map/ppermute | solution.py:149
  51.7 4.8 %collective-permute-done.6 = bf16[4,64,1024]{2,1,0:T(8,128)(2,1)S(1)} collective-permute-done((bf16[4,64,1024]{2,1,0:T(8,128)(2,1)S(1)}, bf16[4,64,1024]{2,1,0:T(8,128)(2,1)S(1)}, u32[]{:S(2)}, u32[]{:S(2)}) %collective-permute-start.6) | collective-permute-done | bytes 524320 | tf_op jit(solution)/shard_map/ppermute | solution.py:149
  56.5 9.4 %collective-permute-start.8 = (bf16[4,64,1024]{2,1,0:T(8,128)(2,1)S(1)}, bf16[4,64,1024]{2,1,0:T(8,128)(2,1)}, u32[]{:S(2)}, u32[]{:S(2)}) collective-permute-start(bf16[4,64,1024]{2,1,0:T(8,128)(2,1)S(1)} %collective-permute-done.6), channel_id=1, source_target_pairs={{0,1},{1,2},{2,3},{3,4},{4,5},{5,6},{6,7},{7,8},{8,9},{9,10},{10,1... | collective-permute-start | bytes 1572872 | tf_op jit(solution)/shard_map/ppermute | solution.py:149
  66.0 2.0 %collective-permute-done.8 = bf16[4,64,1024]{2,1,0:T(8,128)(2,1)} collective-permute-done((bf16[4,64,1024]{2,1,0:T(8,128)(2,1)S(1)}, bf16[4,64,1024]{2,1,0:T(8,128)(2,1)}, u32[]{:S(2)}, u32[]{:S(2)}) %collective-permute-start.8) | collective-permute-done | bytes 524320 | tf_op jit(solution)/shard_map/ppermute | solution.py:149
  68.0 12.1 %collective-permute-start.10 = (bf16[4,64,1024]{2,1,0:T(8,128)(2,1)}, bf16[4,64,1024]{2,1,0:T(8,128)(2,1)}, u32[]{:S(2)}, u32[]{:S(2)}) collective-permute-start(bf16[4,64,1024]{2,1,0:T(8,128)(2,1)} %collective-permute-done.8), channel_id=1, source_target_pairs={{0,1},{1,2},{2,3},{3,4},{4,5},{5,6},{6,7},{7,8},{8,9},{9,10},{10,1... | collective-permute-start | bytes 1572872 | tf_op jit(solution)/shard_map/ppermute | solution.py:149
  80.1 0.8 constant_dynamic-update-slice_fusion.14
  81.8 1.9 %constant_dynamic-update-slice_fusion.12 = bf16[4,1024,1024]{2,1,0:T(8,128)(2,1)} fusion(bf16[4,1024,1024]{2,1,0:T(8,128)(2,1)} %constant_dynamic-update-slice_fusion.13, bf16[4,64,1024]{2,1,0:T(8,128)(2,1)} %copy-done.3, s32[]{:T(128)S(6)} %select_n.146), kind=kLoop, calls=%fused_computation.51 | loop fusion | bytes 1048580 | tf_op jit(solution)/shard_map/dynamic_update_slice | solution.py:150
  83.6 0.8 constant_dynamic-update-slice_fusion.11
  84.5 10.3 %collective-permute-start.12 = (bf16[4,64,1024]{2,1,0:T(8,128)(2,1)}, bf16[4,64,1024]{2,1,0:T(8,128)(2,1)S(1)}, u32[]{:S(2)}, u32[]{:S(2)}) collective-permute-start(bf16[4,64,1024]{2,1,0:T(8,128)(2,1)} %collective-permute-done.10), channel_id=1, source_target_pairs={{0,1},{1,2},{2,3},{3,4},{4,5},{5,6},{6,7},{7,8},{8,9},{9,10},{10,1... | collective-permute-start | bytes 1572872 | tf_op jit(solution)/shard_map/ppermute | solution.py:149
  96.4 1.9 %constant_dynamic-update-slice_fusion.8 = bf16[4,1024,1024]{2,1,0:T(8,128)(2,1)} fusion(bf16[4,1024,1024]{2,1,0:T(8,128)(2,1)} %constant_dynamic-update-slice_fusion.9, bf16[4,64,1024]{2,1,0:T(8,128)(2,1)} %copy-done.2, s32[]{:T(128)S(6)} %select_n.154), kind=kLoop, calls=%fused_computation.47 | loop fusion | bytes 1048580 | tf_op jit(solution)/shard_map/dynamic_update_slice | solution.py:150
  98.3 1.9 %constant_dynamic-update-slice_fusion.7 = bf16[4,1024,1024]{2,1,0:T(8,128)(2,1)} fusion(bf16[4,1024,1024]{2,1,0:T(8,128)(2,1)} %constant_dynamic-update-slice_fusion.8, bf16[4,64,1024]{2,1,0:T(8,128)(2,1)} %collective-permute-done.7, s32[]{:T(128)S(6)} %select_n.156), kind=kLoop, calls=%fused_computation.46 | loop fusion | bytes 1048580 | tf_op jit(solution)/shard_map/dynamic_update_slice | solution.py:155
  100.1 1.9 %constant_dynamic-update-slice_fusion.6 = bf16[4,1024,1024]{2,1,0:T(8,128)(2,1)} fusion(bf16[4,1024,1024]{2,1,0:T(8,128)(2,1)} %constant_dynamic-update-slice_fusion.7, bf16[4,64,1024]{2,1,0:T(8,128)(2,1)} %collective-permute-done.8, s32[]{:T(128)S(6)} %select_n.158), kind=kLoop, calls=%fused_computation.45 | loop fusion | bytes 1048580 | tf_op jit(solution)/shard_map/dynamic_update_slice | solution.py:150
  102.0 7.3 %collective-permute-start.14 = (bf16[4,64,1024]{2,1,0:T(8,128)(2,1)S(1)}, bf16[4,64,1024]{2,1,0:T(8,128)(2,1)S(1)}, u32[]{:S(2)}, u32[]{:S(2)}) collective-permute-start(bf16[4,64,1024]{2,1,0:T(8,128)(2,1)S(1)} %collective-permute-done.12), channel_id=1, source_target_pairs={{0,1},{1,2},{2,3},{3,4},{4,5},{5,6},{6,7},{7,8},{8,9},{9,10},{10,1... | collective-permute-start | bytes 1572872 | tf_op jit(solution)/shard_map/ppermute | solution.py:149
  109.3 0.8 constant_dynamic-update-slice_fusion.5
  110.1 1.9 %constant_dynamic-update-slice_fusion.4 = bf16[4,1024,1024]{2,1,0:T(8,128)(2,1)} fusion(bf16[4,1024,1024]{2,1,0:T(8,128)(2,1)} %constant_dynamic-update-slice_fusion.5, bf16[4,64,1024]{2,1,0:T(8,128)(2,1)} %collective-permute-done.10, s32[]{:T(128)S(6)} %select_n.162), kind=kLoop, calls=%fused_computation.43 | loop fusion | bytes 1048580 | tf_op jit(solution)/shard_map/dynamic_update_slice | solution.py:150
  115.3 3.6 %fusion.27 = (bf16[1,1024,1024]{2,1,0:T(8,128)(2,1)S(1)}, bf16[1,1024,1024]{2,1,0:T(8,128)(2,1)S(1)}, bf16[1,1024,1024]{2,1,0:T(8,128)(2,1)S(1)}) fusion(bf16[4,1024,1024]{2,1,0:T(8,128)(2,1)} %constant_dynamic-update-slice_fusion), kind=kLoop, calls=%fused_computation.59 | loop fusion | bytes 12582912 | tf_op jit(solution)/shard_map/slice | solution.py:159
  118.9 4.6 %negate_convert_fusion = bf16[1024,1024]{1,0:T(8,128)(2,1)S(1)} fusion(bf16[4,1024,1024]{2,1,0:T(8,128)(2,1)} %constant_dynamic-update-slice_fusion), kind=kOutput, calls=%fused_computation | convolution fusion | flops 2149580800 | bytes 6291456 | tf_op jit(solution)/shard_map/dot_general | solution.py:160
  124.7 1.0 fusion.14
  125.7 1.0 fusion.15
  127.4 8.0 %all-to-all-start = ((f32[8,1,512]{2,1,0:T(1,128)}), f32[8,1,512]{2,1,0:T(1,128)S(1)}, u32[]{:S(2)}, u32[]{:S(2)}) async-start(f32[8,1,512]{2,1,0:T(1,128)} %broadcast_in_dim.24), calls=%async_computation | async-start | bytes 32768 | tf_op jit(solution)/shard_map/all_to_all | solution.py:188
  136.1 5.8 %all-to-all-done = f32[8,1,512]{2,1,0:T(1,128)S(1)} async-done(((f32[8,1,512]{2,1,0:T(1,128)}), f32[8,1,512]{2,1,0:T(1,128)S(1)}, u32[]{:S(2)}, u32[]{:S(2)}) %all-to-all-start) | async-done | bytes 16416 | tf_op jit(solution)/shard_map/all_to_all | solution.py:188
  (55 shorter events, 11.3 us)
Async XLA Ops:
  9.9 12.5 %collective-permute-start = (bf16[4,64,1024]{2,1,0:T(8,128)(2,1)S(1)}, bf16[4,64,1024]{2,1,0:T(8,128)(2,1)S(1)}, u32[]{:S(2)}, u32[]{:S(2)}) collective-permute-start(bf16[4,64,1024]{2,1,0:T(8,128)(2,1)S(1)} %get-tuple-element.8), channel_id=1, source_target_pairs={{0,1},{1,2},{2,3},{3,4},{4,5},{5,6},{6,7},{7,8},{8,9},{9,10},{10,1... | collective-permute-start | bytes 1572872 | tf_op jit(solution)/shard_map/ppermute | solution.py:149
  10.3 14.4 %collective-permute-start.1 = (bf16[4,64,1024]{2,1,0:T(8,128)(2,1)S(1)}, bf16[4,64,1024]{2,1,0:T(8,128)(2,1)S(1)}, u32[]{:S(2)}, u32[]{:S(2)}) collective-permute-start(bf16[4,64,1024]{2,1,0:T(8,128)(2,1)S(1)} %get-tuple-element.8), channel_id=1, source_target_pairs={{0,15},{1,0},{2,1},{3,2},{4,3},{5,4},{6,5},{7,6},{8,7},{9,8},{10,9... | collective-permute-start | bytes 1572872 | tf_op jit(solution)/shard_map/ppermute | solution.py:154
  22.3 11.4 %collective-permute-start.2 = (bf16[4,64,1024]{2,1,0:T(8,128)(2,1)S(1)}, bf16[4,64,1024]{2,1,0:T(8,128)(2,1)S(1)}, u32[]{:S(2)}, u32[]{:S(2)}) collective-permute-start(bf16[4,64,1024]{2,1,0:T(8,128)(2,1)S(1)} %collective-permute-done), channel_id=1, source_target_pairs={{0,1},{1,2},{2,3},{3,4},{4,5},{5,6},{6,7},{7,8},{8,9},{9,10},{10,1... | collective-permute-start | bytes 1572872 | tf_op jit(solution)/shard_map/ppermute | solution.py:149
  24.7 13.4 %collective-permute-start.3 = (bf16[4,64,1024]{2,1,0:T(8,128)(2,1)S(1)}, bf16[4,64,1024]{2,1,0:T(8,128)(2,1)S(1)}, u32[]{:S(2)}, u32[]{:S(2)}) collective-permute-start(bf16[4,64,1024]{2,1,0:T(8,128)(2,1)S(1)} %collective-permute-done.1), channel_id=1, source_target_pairs={{0,15},{1,0},{2,1},{3,2},{4,3},{5,4},{6,5},{7,6},{8,7},{9,8},{10,9... | collective-permute-start | bytes 1572872 | tf_op jit(solution)/shard_map/ppermute | solution.py:154
  33.7 32.1 %copy-start.3 = (bf16[4,64,1024]{2,1,0:T(8,128)(2,1)}, bf16[4,64,1024]{2,1,0:T(8,128)(2,1)S(1)}, u32[]{:S(2)}) copy-start(bf16[4,64,1024]{2,1,0:T(8,128)(2,1)S(1)} %collective-permute-done.2) | copy-start | bytes 1572868
  33.8 11.4 %collective-permute-start.4 = (bf16[4,64,1024]{2,1,0:T(8,128)(2,1)S(1)}, bf16[4,64,1024]{2,1,0:T(8,128)(2,1)S(1)}, u32[]{:S(2)}, u32[]{:S(2)}) collective-permute-start(bf16[4,64,1024]{2,1,0:T(8,128)(2,1)S(1)} %collective-permute-done.2), channel_id=1, source_target_pairs={{0,1},{1,2},{2,3},{3,4},{4,5},{5,6},{6,7},{7,8},{8,9},{9,10},{10,1... | collective-permute-start | bytes 1572872 | tf_op jit(solution)/shard_map/ppermute | solution.py:149
  38.2 13.5 %collective-permute-start.5 = (bf16[4,64,1024]{2,1,0:T(8,128)(2,1)S(1)}, bf16[4,64,1024]{2,1,0:T(8,128)(2,1)S(1)}, u32[]{:S(2)}, u32[]{:S(2)}) collective-permute-start(bf16[4,64,1024]{2,1,0:T(8,128)(2,1)S(1)} %collective-permute-done.3), channel_id=1, source_target_pairs={{0,15},{1,0},{2,1},{3,2},{4,3},{5,4},{6,5},{7,6},{8,7},{9,8},{10,9... | collective-permute-start | bytes 1572872 | tf_op jit(solution)/shard_map/ppermute | solution.py:154
  45.2 11.3 %collective-permute-start.6 = (bf16[4,64,1024]{2,1,0:T(8,128)(2,1)S(1)}, bf16[4,64,1024]{2,1,0:T(8,128)(2,1)S(1)}, u32[]{:S(2)}, u32[]{:S(2)}) collective-permute-start(bf16[4,64,1024]{2,1,0:T(8,128)(2,1)S(1)} %collective-permute-done.4), channel_id=1, source_target_pairs={{0,1},{1,2},{2,3},{3,4},{4,5},{5,6},{6,7},{7,8},{8,9},{9,10},{10,1... | collective-permute-start | bytes 1572872 | tf_op jit(solution)/shard_map/ppermute | solution.py:149
  51.7 14.2 %collective-permute-start.7 = (bf16[4,64,1024]{2,1,0:T(8,128)(2,1)S(1)}, bf16[4,64,1024]{2,1,0:T(8,128)(2,1)}, u32[]{:S(2)}, u32[]{:S(2)}) collective-permute-start(bf16[4,64,1024]{2,1,0:T(8,128)(2,1)S(1)} %collective-permute-done.5), channel_id=1, source_target_pairs={{0,15},{1,0},{2,1},{3,2},{4,3},{5,4},{6,5},{7,6},{8,7},{9,8},{10,9... | collective-permute-start | bytes 1572872 | tf_op jit(solution)/shard_map/ppermute | solution.py:154
  56.5 9.4 %copy-start.2 = (bf16[4,64,1024]{2,1,0:T(8,128)(2,1)}, bf16[4,64,1024]{2,1,0:T(8,128)(2,1)S(1)}, u32[]{:S(2)}) copy-start(bf16[4,64,1024]{2,1,0:T(8,128)(2,1)S(1)} %collective-permute-done.6) | copy-start | bytes 1572868
  56.5 11.5 %collective-permute-start.8 = (bf16[4,64,1024]{2,1,0:T(8,128)(2,1)S(1)}, bf16[4,64,1024]{2,1,0:T(8,128)(2,1)}, u32[]{:S(2)}, u32[]{:S(2)}) collective-permute-start(bf16[4,64,1024]{2,1,0:T(8,128)(2,1)S(1)} %collective-permute-done.6), channel_id=1, source_target_pairs={{0,1},{1,2},{2,3},{3,4},{4,5},{5,6},{6,7},{7,8},{8,9},{9,10},{10,1... | collective-permute-start | bytes 1572872 | tf_op jit(solution)/shard_map/ppermute | solution.py:149
  65.9 17.7 %collective-permute-start.9 = (bf16[4,64,1024]{2,1,0:T(8,128)(2,1)}, bf16[4,64,1024]{2,1,0:T(8,128)(2,1)S(1)}, u32[]{:S(2)}, u32[]{:S(2)}) collective-permute-start(bf16[4,64,1024]{2,1,0:T(8,128)(2,1)} %collective-permute-done.7), channel_id=1, source_target_pairs={{0,15},{1,0},{2,1},{3,2},{4,3},{5,4},{6,5},{7,6},{8,7},{9,8},{10,9... | collective-permute-start | bytes 1572872 | tf_op jit(solution)/shard_map/ppermute | solution.py:154
  68.0 16.5 %collective-permute-start.10 = (bf16[4,64,1024]{2,1,0:T(8,128)(2,1)}, bf16[4,64,1024]{2,1,0:T(8,128)(2,1)}, u32[]{:S(2)}, u32[]{:S(2)}) collective-permute-start(bf16[4,64,1024]{2,1,0:T(8,128)(2,1)} %collective-permute-done.8), channel_id=1, source_target_pairs={{0,1},{1,2},{2,3},{3,4},{4,5},{5,6},{6,7},{7,8},{8,9},{9,10},{10,1... | collective-permute-start | bytes 1572872 | tf_op jit(solution)/shard_map/ppermute | solution.py:149
  83.6 16.5 %collective-permute-start.11 = (bf16[4,64,1024]{2,1,0:T(8,128)(2,1)S(1)}, bf16[4,64,1024]{2,1,0:T(8,128)(2,1)S(1)}, u32[]{:S(2)}, u32[]{:S(2)}) collective-permute-start(bf16[4,64,1024]{2,1,0:T(8,128)(2,1)S(1)} %collective-permute-done.9), channel_id=1, source_target_pairs={{0,15},{1,0},{2,1},{3,2},{4,3},{5,4},{6,5},{7,6},{8,7},{9,8},{10,9... | collective-permute-start | bytes 1572872 | tf_op jit(solution)/shard_map/ppermute | solution.py:154
  84.5 17.5 %collective-permute-start.12 = (bf16[4,64,1024]{2,1,0:T(8,128)(2,1)}, bf16[4,64,1024]{2,1,0:T(8,128)(2,1)S(1)}, u32[]{:S(2)}, u32[]{:S(2)}) collective-permute-start(bf16[4,64,1024]{2,1,0:T(8,128)(2,1)} %collective-permute-done.10), channel_id=1, source_target_pairs={{0,1},{1,2},{2,3},{3,4},{4,5},{5,6},{6,7},{7,8},{8,9},{9,10},{10,1... | collective-permute-start | bytes 1572872 | tf_op jit(solution)/shard_map/ppermute | solution.py:149
  100.1 13.5 %collective-permute-start.13 = (bf16[4,64,1024]{2,1,0:T(8,128)(2,1)S(1)}, bf16[4,64,1024]{2,1,0:T(8,128)(2,1)S(1)}, u32[]{:S(2)}, u32[]{:S(2)}) collective-permute-start(bf16[4,64,1024]{2,1,0:T(8,128)(2,1)S(1)} %collective-permute-done.11), channel_id=1, source_target_pairs={{0,15},{1,0},{2,1},{3,2},{4,3},{5,4},{6,5},{7,6},{8,7},{9,8},{10,9... | collective-permute-start | bytes 1572872 | tf_op jit(solution)/shard_map/ppermute | solution.py:154
  102.0 12.5 %collective-permute-start.14 = (bf16[4,64,1024]{2,1,0:T(8,128)(2,1)S(1)}, bf16[4,64,1024]{2,1,0:T(8,128)(2,1)S(1)}, u32[]{:S(2)}, u32[]{:S(2)}) collective-permute-start(bf16[4,64,1024]{2,1,0:T(8,128)(2,1)S(1)} %collective-permute-done.12), channel_id=1, source_target_pairs={{0,1},{1,2},{2,3},{3,4},{4,5},{5,6},{6,7},{7,8},{8,9},{9,10},{10,1... | collective-permute-start | bytes 1572872 | tf_op jit(solution)/shard_map/ppermute | solution.py:149
  118.8 4.7 %copy-start.1 = (bf16[128,1024]{1,0:T(8,128)(2,1)S(1)}, bf16[128,1024]{1,0:T(8,128)(2,1)}, u32[]{:S(2)}) copy-start(bf16[128,1024]{1,0:T(8,128)(2,1)} %param.8) | copy-start | bytes 786436
  118.9 5.3 %copy-start.4 = (f32[128,1024]{1,0:T(8,128)S(1)}, f32[128,1024]{1,0:T(8,128)}, u32[]{:S(2)}) copy-start(f32[128,1024]{1,0:T(8,128)} %param.9) | copy-start | bytes 1572868
  123.5 18.5 %copy-start.5 = (f32[512]{0:T(512)S(1)}, f32[512]{0:T(512)}, u32[]{:S(2)}) copy-start(f32[512]{0:T(512)} %param.15) | copy-start | bytes 6148
  124.7 17.9 %copy-start = (f32[128,1024]{1,0:T(8,128)}, f32[128,1024]{1,0:T(8,128)S(1)}, u32[]{:S(2)}) copy-start(f32[128,1024]{1,0:T(8,128)S(1)} %convolution_subtract_fusion) | copy-start | bytes 1572868
  127.4 14.6 %all-to-all-start = ((f32[8,1,512]{2,1,0:T(1,128)}), f32[8,1,512]{2,1,0:T(1,128)S(1)}, u32[]{:S(2)}, u32[]{:S(2)}) async-start(f32[8,1,512]{2,1,0:T(1,128)} %broadcast_in_dim.24), calls=%async_computation | async-start | bytes 32768 | tf_op jit(solution)/shard_map/all_to_all | solution.py:188
